TPU v7x, 512 devices: a whole 4x8x8 slice. The times are simulated.
512 devices in a mesh: shift: 4 (over x_hi, core), space: 128 (over y, z, x_lo).
Axes of the slice: x: 4 (x_hi: 2, x_lo: 2; x = x_hi * 2 + x_lo), y: 8, z: 8, core: 2. Of those that a mesh axis runs over, the one named last changes fastest.
Arguments:
- labels: int32 [256, 32, 256], P('space'), may hold values from 0 to 7
- conductance: float32 [8], replicated, may hold values from 0.2 to 5
- capacity_table: float32 [8], replicated, may hold values from 0.5 to 2
- shift_values: float32 [8], replicated, may hold values from 0.1 to 4
- prior_basis: float32 [256, 256, 32, 256], P(None, 'space', 'shift'), may hold values from -6 to 6
Outputs:
- new_block: float32 [8, 8, 256, 32, 256], P(None, None, 'space', 'shift')
- coefficients: float32 [64, 256], replicated
- factor: float32 [64, 64], replicated
All inputs are finite; a program needn't handle non-finite values.
Results may differ from a plain program's by a relative error of at most 0.0003.
Values sent between devices are 32-bit elements; how exact they have to be, the bound alone decides.
No kernel may reach another device: no remote copies, remote signals or barrier semaphores. Data moves between devices by JAX's collectives and lax.ppermute only.
A program may use at most 64 MiB of HBM per device.

v0:
```python
import jax
import jax.numpy as jnp
from jax import lax
from jax.sharding import PartitionSpec as P

COLS = 8
SWEEPS = 4
LOWER_BOUND = 0.1
UPPER_BOUND = 2.0


def padded_2(cells, sides, width):
    for axis, dim in sides:
        count = lax.axis_size(axis)
        ends = count - 1
        head = lax.slice_in_dim(cells, 0, width, axis=dim)
        tail = lax.slice_in_dim(cells, cells.shape[dim] - width, cells.shape[dim], axis=dim)
        cells = jnp.concatenate(
            [
                lax.ppermute(tail, axis, [(i, (i + 1) % count) for i in range(ends)]),
                cells,
                lax.ppermute(head, axis, [((i + 1) % count, i) for i in range(ends)]),
            ],
            axis=dim,
        )
    return cells


def allsum(value):
    axes = ("shift", "space")
    total = lax.axis_size("shift") * lax.axis_size("space")
    if total & total - 1:
        return lax.psum(value, axes)
    for bit in range(total.bit_length() - 1):
        mask = 1 << bit
        value = value + lax.ppermute(value, axes, [(i, i ^ mask) for i in range(total)])
    return value


def lookup(labels, table):
    materials = jnp.arange(table.shape[0], dtype=jnp.int32)
    onehot = (labels[None] == materials[:, None, None, None]).astype(jnp.float32)
    return jnp.sum(onehot * table[:, None, None, None], axis=0)


def conductances(conduct, padded):
    west_face = 0.5 * (conduct + padded[:-2, 1:-1, 1:-1])
    east_face = 0.5 * (conduct + padded[2:, 1:-1, 1:-1])
    south_face = 0.5 * (conduct + padded[1:-1, :-2, 1:-1])
    north_face = 0.5 * (conduct + padded[1:-1, 2:, 1:-1])
    below_face = 0.5 * (conduct + padded[1:-1, 1:-1, :-2])
    above_face = 0.5 * (conduct + padded[1:-1, 1:-1, 2:])
    return (west_face, east_face, south_face, north_face, below_face, above_face)


def neighbours(padded, face_list):
    west_face, east_face, south_face, north_face, below_face, above_face = face_list
    summed = west_face * padded[..., :-2, 1:-1, 1:-1] + east_face * padded[..., 2:, 1:-1, 1:-1]
    summed = (
        summed
        + south_face * padded[..., 1:-1, :-2, 1:-1]
        + north_face * padded[..., 1:-1, 2:, 1:-1]
    )
    summed = (
        summed
        + below_face * padded[..., 1:-1, 1:-1, :-2]
        + above_face * padded[..., 1:-1, 1:-1, 2:]
    )
    return summed


def diagonal_of(face_list, shift_list, capacity):
    west_face, east_face, south_face, north_face, below_face, above_face = face_list
    summed = west_face + east_face + (south_face + north_face) + (below_face + above_face)
    return summed[None, None] + shift_list[:, None, None, None, None] * capacity[None, None]


def chebyshev(source, face_list, diagonal, padder):
    center = 0.5 * (UPPER_BOUND + LOWER_BOUND)
    spread = 0.5 * (UPPER_BOUND - LOWER_BOUND)
    ratio_value = center / spread
    reciprocal = 1.0 / diagonal
    solution = jnp.zeros_like(source)
    remainder = source
    weight_old = 1.0 / ratio_value
    direction = reciprocal * remainder / center
    for sweep_index in range(SWEEPS):
        solution = solution + direction
        if sweep_index + 1 < SWEEPS:
            applied = diagonal * direction - neighbours(padder(direction), face_list)
            remainder = remainder - applied
            weight_new = 1.0 / (2.0 * ratio_value - weight_old)
            direction = weight_new * weight_old * direction + 2.0 * weight_new / spread * (
                reciprocal * remainder
            )
            weight_old = weight_new
    return solution


def products(left_side, right_side):
    return lax.dot_general(
        left_side, right_side, (((1,), (1,)), ((), ())), precision=lax.Precision.HIGHEST
    )


def matmul(left_side, right_side):
    return jnp.dot(left_side, right_side, precision=lax.Precision.HIGHEST)


def local(labels, conductance, capacity_table, shift_values, prior_basis):
    groups = lax.axis_size("shift")
    shifts_all = shift_values.shape[0]
    per_device = shifts_all // groups
    new_count = shifts_all * COLS
    basis_count = prior_basis.shape[0]
    slab_x = prior_basis.shape[1]
    quarter = prior_basis.shape[2]
    depth = prior_basis.shape[3]
    flat_basis = prior_basis.reshape(basis_count, slab_x * quarter * depth)
    cell_weight = 1.0 / (slab_x * quarter * depth * groups * lax.axis_size("space"))
    tail_columns = prior_basis[basis_count - new_count :]
    conduct = lookup(labels, conductance)
    capacity = lookup(labels, capacity_table)
    rimmed = padded_2(conduct, (("space", 0),), 1)
    face_list = conductances(conduct, jnp.pad(rimmed, ((0, 0), (1, 1), (1, 1))))
    shift_list = lax.dynamic_slice_in_dim(
        shift_values, lax.axis_index("shift") * per_device, per_device, 0
    )
    diagonal = diagonal_of(face_list, shift_list, capacity)
    starting = lax.all_to_all(tail_columns, "shift", split_axis=0, concat_axis=2, tiled=True)
    full_y = starting.shape[2]
    source = starting.reshape(per_device, COLS, slab_x, full_y, depth) * capacity[None, None]

    def padder(field):
        widened = padded_2(field, (("space", 2),), 1)
        return jnp.pad(widened, ((0, 0), (0, 0), (0, 0), (1, 1), (1, 1)))

    fields = chebyshev(source, face_list, diagonal, padder)
    merged = fields.reshape(per_device * COLS, slab_x, full_y, depth)
    regrouped = lax.all_to_all(merged, "shift", split_axis=2, concat_axis=0, tiled=True)
    columns = regrouped.reshape(new_count, slab_x * quarter * depth)
    first_proj = allsum(products(columns, flat_basis)) * cell_weight
    columns = columns - matmul(first_proj, flat_basis)
    second_proj = allsum(products(columns, flat_basis)) * cell_weight
    columns = columns - matmul(second_proj, flat_basis)
    gram_matrix = allsum(products(columns, columns)) * cell_weight
    factor = jnp.linalg.cholesky(gram_matrix)
    orthonormal = lax.linalg.triangular_solve(factor, columns, left_side=True, lower=True)
    new_block = orthonormal.reshape(shifts_all, COLS, slab_x, quarter, depth)
    return (new_block, first_proj + second_proj, factor)


def solution(mesh):
    in_specs = (P("space", None, None), P(), P(), P(), P(None, "space", "shift", None))
    out_specs = (P(None, None, "space", "shift", None), P(), P())
    return jax.shard_map(local, mesh=mesh, in_specs=in_specs, out_specs=out_specs, check_vma=False)
```

profile of v0, /device:TPU:56, one launch (start us, length us, event | category | flops | bytes accessed | tf_op | source)
XLA Modules:
  0.0 369.8 jit_solution(17943943880740314780)
XLA Ops:
  3.0 4.3 %all-to-all-start = ((f32[64,2,8,256]{3,2,1,0:T(8,128)}), f32[64,2,8,256]{3,2,1,0:T(8,128)S(1)}, u32[]{:S(2)}, u32[]{:S(2)}) async-start(f32[64,2,8,256]{3,2,1,0:T(8,128)} %slice.133), calls=%async_computation | async-start | bytes 2097152 | tf_op jit(solution)/shard_map/all_to_all | solution.py:130
  10.1 11.2 %collective-permute-start.1 = (f32[1,32,256]{2,1,0:T(8,128)S(1)}, f32[1,32,256]{2,1,0:T(8,128)S(1)}, u32[]{:S(2)}, u32[]{:S(2)}) collective-permute-start(f32[1,32,256]{2,1,0:T(8,128)S(1)} %get-tuple-element.43), channel_id=1, source_target_pairs={{1,0},{2,1},{3,2},{4,3},{5,4},{6,5},{7,6},{8,7},{9,8},{10,9},{11,1... | collective-permute-start | bytes 98312 | tf_op jit(solution)/shard_map/ppermute | solution.py:22
  27.3 11.2 %collective-permute-start.3 = (f32[2,8,1,32,256]{4,3,2,1,0:T(8,128)S(1)}, f32[2,8,1,32,256]{4,3,2,1,0:T(8,128)S(1)}, u32[]{:S(2)}, u32[]{:S(2)}) collective-permute-start(f32[2,8,1,32,256]{4,3,2,1,0:T(8,128)S(1)} %get-tuple-element.38), channel_id=1, source_target_pairs={{1,0},{2,1},{3,2},{4,3},{5,4},{6,5},{7,6},{8,7},{9,8},{10,9},{11,1... | collective-permute-start | bytes 1572872 | tf_op jit(solution)/shard_map/ppermute | solution.py:22
  38.5 10.3 %collective-permute-done.2 = f32[2,8,1,32,256]{4,3,2,1,0:T(8,128)S(1)} collective-permute-done((f32[2,8,1,32,256]{4,3,2,1,0:T(8,128)S(1)}, f32[2,8,1,32,256]{4,3,2,1,0:T(8,128)S(1)}, u32[]{:S(2)}, u32[]{:S(2)}) %collective-permute-start.2) | collective-permute-done | bytes 524320 | tf_op jit(solution)/shard_map/ppermute | solution.py:20
  48.7 5.9 %collective-permute-done.3 = f32[2,8,1,32,256]{4,3,2,1,0:T(8,128)S(1)} collective-permute-done((f32[2,8,1,32,256]{4,3,2,1,0:T(8,128)S(1)}, f32[2,8,1,32,256]{4,3,2,1,0:T(8,128)S(1)}, u32[]{:S(2)}, u32[]{:S(2)}) %collective-permute-start.3) | collective-permute-done | bytes 524320 | tf_op jit(solution)/shard_map/ppermute | solution.py:22
  59.7 8.1 %collective-permute-start.5 = (f32[2,8,1,32,256]{4,3,2,1,0:T(8,128)S(1)}, f32[2,8,1,32,256]{4,3,2,1,0:T(8,128)S(1)}, u32[]{:S(2)}, u32[]{:S(2)}) collective-permute-start(f32[2,8,1,32,256]{4,3,2,1,0:T(8,128)S(1)} %get-tuple-element.36), channel_id=1, source_target_pairs={{1,0},{2,1},{3,2},{4,3},{5,4},{6,5},{7,6},{8,7},{9,8},{10,9},{11,1... | collective-permute-start | bytes 1572872 | tf_op jit(solution)/shard_map/ppermute | solution.py:22
  67.9 13.1 %collective-permute-done.4 = f32[2,8,1,32,256]{4,3,2,1,0:T(8,128)S(1)} collective-permute-done((f32[2,8,1,32,256]{4,3,2,1,0:T(8,128)S(1)}, f32[2,8,1,32,256]{4,3,2,1,0:T(8,128)S(1)}, u32[]{:S(2)}, u32[]{:S(2)}) %collective-permute-start.4) | collective-permute-done | bytes 524320 | tf_op jit(solution)/shard_map/ppermute | solution.py:20
  80.9 4.7 %collective-permute-done.5 = f32[2,8,1,32,256]{4,3,2,1,0:T(8,128)S(1)} collective-permute-done((f32[2,8,1,32,256]{4,3,2,1,0:T(8,128)S(1)}, f32[2,8,1,32,256]{4,3,2,1,0:T(8,128)S(1)}, u32[]{:S(2)}, u32[]{:S(2)}) %collective-permute-start.5) | collective-permute-done | bytes 524320 | tf_op jit(solution)/shard_map/ppermute | solution.py:22
  90.7 7.9 %collective-permute-start.7 = (f32[2,8,1,32,256]{4,3,2,1,0:T(8,128)S(1)}, f32[2,8,1,32,256]{4,3,2,1,0:T(8,128)S(1)}, u32[]{:S(2)}, u32[]{:S(2)}) collective-permute-start(f32[2,8,1,32,256]{4,3,2,1,0:T(8,128)S(1)} %get-tuple-element.34), channel_id=1, source_target_pairs={{1,0},{2,1},{3,2},{4,3},{5,4},{6,5},{7,6},{8,7},{9,8},{10,9},{11,1... | collective-permute-start | bytes 1572872 | tf_op jit(solution)/shard_map/ppermute | solution.py:22
  98.6 13.0 %collective-permute-done.6 = f32[2,8,1,32,256]{4,3,2,1,0:T(8,128)S(1)} collective-permute-done((f32[2,8,1,32,256]{4,3,2,1,0:T(8,128)S(1)}, f32[2,8,1,32,256]{4,3,2,1,0:T(8,128)S(1)}, u32[]{:S(2)}, u32[]{:S(2)}) %collective-permute-start.6) | collective-permute-done | bytes 524320 | tf_op jit(solution)/shard_map/ppermute | solution.py:20
  111.6 5.0 %collective-permute-done.7 = f32[2,8,1,32,256]{4,3,2,1,0:T(8,128)S(1)} collective-permute-done((f32[2,8,1,32,256]{4,3,2,1,0:T(8,128)S(1)}, f32[2,8,1,32,256]{4,3,2,1,0:T(8,128)S(1)}, u32[]{:S(2)}, u32[]{:S(2)}) %collective-permute-start.7) | collective-permute-done | bytes 524320 | tf_op jit(solution)/shard_map/ppermute | solution.py:22
  125.3 8.0 %copy.51 = f32[32,8,16,256]{3,1,2,0:T(8,128)} copy(f32[32,8,16,256]{3,2,1,0:T(8,128)} %bitcast.53) | data formatting | bytes 8388608
  133.3 7.8 %all-to-all-done.1 = f32[16,2,32,256]{3,1,0,2:T(2,128)S(1)} async-done(((f32[16,2,32,256]{3,1,0,2:T(2,128)}), f32[16,2,32,256]{3,1,0,2:T(2,128)S(1)}, u32[]{:S(2)}, u32[]{:S(2)}) %all-to-all-start.1) | async-done | bytes 1048608 | tf_op jit(solution)/shard_map/all_to_all | solution.py:140
  142.1 6.3 %fusion.68 = f32[64,256]{1,0:T(8,128)S(1)} fusion(f32[64,4096]{1,0:T(8,128)S(1)} %reshape.60, f32[256,4096]{1,0:T(8,128)} %bitcast.45), kind=kOutput, calls=%fused_computation.121 | convolution fusion | flops 805306368 | bytes 5308416 | tf_op jit(solution)/shard_map/dot_general | solution.py:101
  150.3 4.2 %collective-permute-done.8 = f32[64,256]{1,0:T(8,128)S(1)} collective-permute-done((f32[64,256]{1,0:T(8,128)S(1)}, f32[64,256]{1,0:T(8,128)S(1)}, u32[]{:S(2)}, u32[]{:S(2)}) %collective-permute-start.8) | collective-permute-done | bytes 65568 | tf_op jit(solution)/shard_map/ppermute | solution.py:36
  156.4 4.2 %collective-permute-done.9 = f32[64,256]{1,0:T(8,128)S(1)} collective-permute-done((f32[64,256]{1,0:T(8,128)S(1)}, f32[64,256]{1,0:T(8,128)S(1)}, u32[]{:S(2)}, u32[]{:S(2)}) %collective-permute-start.9) | collective-permute-done | bytes 65568 | tf_op jit(solution)/shard_map/ppermute | solution.py:36
  164.2 4.3 %collective-permute-done.10 = f32[64,256]{1,0:T(8,128)S(1)} collective-permute-done((f32[64,256]{1,0:T(8,128)S(1)}, f32[64,256]{1,0:T(8,128)S(1)}, u32[]{:S(2)}, u32[]{:S(2)}) %collective-permute-start.10) | collective-permute-done | bytes 65568 | tf_op jit(solution)/shard_map/ppermute | solution.py:36
  168.5 11.3 %collective-permute-start.11 = (f32[64,256]{1,0:T(8,128)S(1)}, f32[64,256]{1,0:T(8,128)S(1)}, u32[]{:S(2)}, u32[]{:S(2)}) collective-permute-start(f32[64,256]{1,0:T(8,128)S(1)} %add.255), channel_id=1, source_target_pairs={{0,8},{1,9},{2,10},{3,11},{4,12},{5,13},{6,14},{7,15},{8,0},{9,1},... | collective-permute-start | bytes 196616 | tf_op jit(solution)/shard_map/ppermute | solution.py:36
  196.0 4.7 %collective-permute-start.14 = (f32[64,256]{1,0:T(8,128)S(1)}, f32[64,256]{1,0:T(8,128)S(1)}, u32[]{:S(2)}, u32[]{:S(2)}) collective-permute-start(f32[64,256]{1,0:T(8,128)S(1)} %add.258), channel_id=1, source_target_pairs={{0,64},{1,65},{2,66},{3,67},{4,68},{5,69},{6,70},{7,71},{8,72},{9,... | collective-permute-start | bytes 196616 | tf_op jit(solution)/shard_map/ppermute | solution.py:36
  200.7 6.0 %collective-permute-done.14 = f32[64,256]{1,0:T(8,128)S(1)} collective-permute-done((f32[64,256]{1,0:T(8,128)S(1)}, f32[64,256]{1,0:T(8,128)S(1)}, u32[]{:S(2)}, u32[]{:S(2)}) %collective-permute-start.14) | collective-permute-done | bytes 65568 | tf_op jit(solution)/shard_map/ppermute | solution.py:36
  212.4 5.1 %collective-permute-done.16 = f32[64,256]{1,0:T(8,128)S(1)} collective-permute-done((f32[64,256]{1,0:T(8,128)S(1)}, f32[64,256]{1,0:T(8,128)S(1)}, u32[]{:S(2)}, u32[]{:S(2)}) %collective-permute-start.16) | collective-permute-done | bytes 65568 | tf_op jit(solution)/shard_map/ppermute | solution.py:36
  232.3 4.2 %collective-permute-done.18 = f32[64,256]{1,0:T(8,128)S(1)} collective-permute-done((f32[64,256]{1,0:T(8,128)S(1)}, f32[64,256]{1,0:T(8,128)S(1)}, u32[]{:S(2)}, u32[]{:S(2)}) %collective-permute-start.18) | collective-permute-done | bytes 65568 | tf_op jit(solution)/shard_map/ppermute | solution.py:36
  238.4 5.3 %collective-permute-done.19 = f32[64,256]{1,0:T(8,128)S(1)} collective-permute-done((f32[64,256]{1,0:T(8,128)S(1)}, f32[64,256]{1,0:T(8,128)S(1)}, u32[]{:S(2)}, u32[]{:S(2)}) %collective-permute-start.19) | collective-permute-done | bytes 65568 | tf_op jit(solution)/shard_map/ppermute | solution.py:36
  243.7 8.0 %collective-permute-start.20 = (f32[64,256]{1,0:T(8,128)S(1)}, f32[64,256]{1,0:T(8,128)S(1)}, u32[]{:S(2)}, u32[]{:S(2)}) collective-permute-start(f32[64,256]{1,0:T(8,128)S(1)} %add.264), channel_id=1, source_target_pairs={{0,8},{1,9},{2,10},{3,11},{4,12},{5,13},{6,14},{7,15},{8,0},{9,1},... | collective-permute-start | bytes 196616 | tf_op jit(solution)/shard_map/ppermute | solution.py:36
  264.1 4.4 %collective-permute-done.22 = f32[64,256]{1,0:T(8,128)S(1)} collective-permute-done((f32[64,256]{1,0:T(8,128)S(1)}, f32[64,256]{1,0:T(8,128)S(1)}, u32[]{:S(2)}, u32[]{:S(2)}) %collective-permute-start.22) | collective-permute-done | bytes 65568 | tf_op jit(solution)/shard_map/ppermute | solution.py:36
  272.2 6.4 %collective-permute-done.23 = f32[64,256]{1,0:T(8,128)S(1)} collective-permute-done((f32[64,256]{1,0:T(8,128)S(1)}, f32[64,256]{1,0:T(8,128)S(1)}, u32[]{:S(2)}, u32[]{:S(2)}) %collective-permute-start.23) | collective-permute-done | bytes 65568 | tf_op jit(solution)/shard_map/ppermute | solution.py:36
  284.3 5.1 %collective-permute-done.25 = f32[64,256]{1,0:T(8,128)S(1)} collective-permute-done((f32[64,256]{1,0:T(8,128)S(1)}, f32[64,256]{1,0:T(8,128)S(1)}, u32[]{:S(2)}, u32[]{:S(2)}) %collective-permute-start.25) | collective-permute-done | bytes 65568 | tf_op jit(solution)/shard_map/ppermute | solution.py:36
  306.6 5.0 %collective-permute-done.28 = f32[64,64]{0,1:T(8,128)S(1)} collective-permute-done((f32[64,64]{0,1:T(8,128)S(1)}, f32[64,64]{0,1:T(8,128)S(1)}, u32[]{:S(2)}, u32[]{:S(2)}) %collective-permute-start.28) | collective-permute-done | bytes 16416 | tf_op jit(solution)/shard_map/ppermute | solution.py:36
  311.6 7.6 %collective-permute-start.29 = (f32[64,64]{0,1:T(8,128)S(1)}, f32[64,64]{0,1:T(8,128)S(1)}, u32[]{:S(2)}, u32[]{:S(2)}) collective-permute-start(f32[64,64]{0,1:T(8,128)S(1)} %add.273), channel_id=1, source_target_pairs={{0,8},{1,9},{2,10},{3,11},{4,12},{5,13},{6,14},{7,15},{8,0},{9,1},... | collective-permute-start | bytes 49160 | tf_op jit(solution)/shard_map/ppermute | solution.py:36
  337.6 6.0 %collective-permute-done.32 = f32[64,64]{0,1:T(8,128)S(1)} collective-permute-done((f32[64,64]{0,1:T(8,128)S(1)}, f32[64,64]{0,1:T(8,128)S(1)}, u32[]{:S(2)}, u32[]{:S(2)}) %collective-permute-start.32) | collective-permute-done | bytes 16416 | tf_op jit(solution)/shard_map/ppermute | solution.py:36
  354.1 5.8 %cholesky.16 = f32[64,64]{1,0:T(8,128)S(1)} custom-call(f32[64,64]{1,0:T(8,128)S(1)} %fusion.52), custom_call_target="Cholesky" | custom-call | tf_op jit(solution)/shard_map/jit(cholesky)/cholesky | solution.py:147
  361.9 4.9 %custom-call.6 = f32[1,64,64]{1,2,0:T(8,128)S(1)} custom-call(f32[1,64,64]{2,1,0:T(8,128)S(1)} %get-tuple-element.20), custom_call_target="InvertDiagBlocksLowerTriangular" | custom-call | tf_op jit(solution)/shard_map/triangular_solve | solution.py:148
  (117 shorter events, 149.1 us)
Async XLA Ops:
  3.0 21.3 %all-to-all-start = ((f32[64,2,8,256]{3,2,1,0:T(8,128)}), f32[64,2,8,256]{3,2,1,0:T(8,128)S(1)}, u32[]{:S(2)}, u32[]{:S(2)}) async-start(f32[64,2,8,256]{3,2,1,0:T(8,128)} %slice.133), calls=%async_computation | async-start | bytes 2097152 | tf_op jit(solution)/shard_map/all_to_all | solution.py:130
  7.5 14.0 %collective-permute-start = (f32[1,32,256]{2,1,0:T(8,128)S(1)}, f32[1,32,256]{2,1,0:T(8,128)S(1)}, u32[]{:S(2)}, u32[]{:S(2)}) collective-permute-start(f32[1,32,256]{2,1,0:T(8,128)S(1)} %get-tuple-element.42), channel_id=1, source_target_pairs={{0,1},{1,2},{2,3},{3,4},{4,5},{5,6},{6,7},{7,8},{8,9},{9,10},{10,1... | collective-permute-start | bytes 98312 | tf_op jit(solution)/shard_map/ppermute | solution.py:20
  10.1 12.8 %collective-permute-start.1 = (f32[1,32,256]{2,1,0:T(8,128)S(1)}, f32[1,32,256]{2,1,0:T(8,128)S(1)}, u32[]{:S(2)}, u32[]{:S(2)}) collective-permute-start(f32[1,32,256]{2,1,0:T(8,128)S(1)} %get-tuple-element.43), channel_id=1, source_target_pairs={{1,0},{2,1},{3,2},{4,3},{5,4},{6,5},{7,6},{8,7},{9,8},{10,9},{11,1... | collective-permute-start | bytes 98312 | tf_op jit(solution)/shard_map/ppermute | solution.py:22
  24.7 24.1 %collective-permute-start.2 = (f32[2,8,1,32,256]{4,3,2,1,0:T(8,128)S(1)}, f32[2,8,1,32,256]{4,3,2,1,0:T(8,128)S(1)}, u32[]{:S(2)}, u32[]{:S(2)}) collective-permute-start(f32[2,8,1,32,256]{4,3,2,1,0:T(8,128)S(1)} %get-tuple-element.37), channel_id=1, source_target_pairs={{0,1},{1,2},{2,3},{3,4},{4,5},{5,6},{6,7},{7,8},{8,9},{9,10},{10,1... | collective-permute-start | bytes 1572872 | tf_op jit(solution)/shard_map/ppermute | solution.py:20
  27.3 27.4 %collective-permute-start.3 = (f32[2,8,1,32,256]{4,3,2,1,0:T(8,128)S(1)}, f32[2,8,1,32,256]{4,3,2,1,0:T(8,128)S(1)}, u32[]{:S(2)}, u32[]{:S(2)}) collective-permute-start(f32[2,8,1,32,256]{4,3,2,1,0:T(8,128)S(1)} %get-tuple-element.38), channel_id=1, source_target_pairs={{1,0},{2,1},{3,2},{4,3},{5,4},{6,5},{7,6},{8,7},{9,8},{10,9},{11,1... | collective-permute-start | bytes 1572872 | tf_op jit(solution)/shard_map/ppermute | solution.py:22
  57.8 23.1 %collective-permute-start.4 = (f32[2,8,1,32,256]{4,3,2,1,0:T(8,128)S(1)}, f32[2,8,1,32,256]{4,3,2,1,0:T(8,128)S(1)}, u32[]{:S(2)}, u32[]{:S(2)}) collective-permute-start(f32[2,8,1,32,256]{4,3,2,1,0:T(8,128)S(1)} %get-tuple-element.35), channel_id=1, source_target_pairs={{0,1},{1,2},{2,3},{3,4},{4,5},{5,6},{6,7},{7,8},{8,9},{9,10},{10,1... | collective-permute-start | bytes 1572872 | tf_op jit(solution)/shard_map/ppermute | solution.py:20
  59.7 25.9 %collective-permute-start.5 = (f32[2,8,1,32,256]{4,3,2,1,0:T(8,128)S(1)}, f32[2,8,1,32,256]{4,3,2,1,0:T(8,128)S(1)}, u32[]{:S(2)}, u32[]{:S(2)}) collective-permute-start(f32[2,8,1,32,256]{4,3,2,1,0:T(8,128)S(1)} %get-tuple-element.36), channel_id=1, source_target_pairs={{1,0},{2,1},{3,2},{4,3},{5,4},{6,5},{7,6},{8,7},{9,8},{10,9},{11,1... | collective-permute-start | bytes 1572872 | tf_op jit(solution)/shard_map/ppermute | solution.py:22
  88.8 22.8 %collective-permute-start.6 = (f32[2,8,1,32,256]{4,3,2,1,0:T(8,128)S(1)}, f32[2,8,1,32,256]{4,3,2,1,0:T(8,128)S(1)}, u32[]{:S(2)}, u32[]{:S(2)}) collective-permute-start(f32[2,8,1,32,256]{4,3,2,1,0:T(8,128)S(1)} %get-tuple-element.33), channel_id=1, source_target_pairs={{0,1},{1,2},{2,3},{3,4},{4,5},{5,6},{6,7},{7,8},{8,9},{9,10},{10,1... | collective-permute-start | bytes 1572872 | tf_op jit(solution)/shard_map/ppermute | solution.py:20
  90.7 26.0 %collective-permute-start.7 = (f32[2,8,1,32,256]{4,3,2,1,0:T(8,128)S(1)}, f32[2,8,1,32,256]{4,3,2,1,0:T(8,128)S(1)}, u32[]{:S(2)}, u32[]{:S(2)}) collective-permute-start(f32[2,8,1,32,256]{4,3,2,1,0:T(8,128)S(1)} %get-tuple-element.34), channel_id=1, source_target_pairs={{1,0},{2,1},{3,2},{4,3},{5,4},{6,5},{7,6},{8,7},{9,8},{10,9},{11,1... | collective-permute-start | bytes 1572872 | tf_op jit(solution)/shard_map/ppermute | solution.py:22
  121.6 19.5 %all-to-all-start.1 = ((f32[16,2,32,256]{3,1,0,2:T(2,128)}), f32[16,2,32,256]{3,1,0,2:T(2,128)S(1)}, u32[]{:S(2)}, u32[]{:S(2)}) async-start(f32[16,2,32,256]{3,1,0,2:T(2,128)} %copy.40), calls=%async_computation.1 | async-start | bytes 2097152 | tf_op jit(solution)/shard_map/all_to_all | solution.py:140
  148.3 6.2 %collective-permute-start.8 = (f32[64,256]{1,0:T(8,128)S(1)}, f32[64,256]{1,0:T(8,128)S(1)}, u32[]{:S(2)}, u32[]{:S(2)}) collective-permute-start(f32[64,256]{1,0:T(8,128)S(1)} %fusion.68), channel_id=1, source_target_pairs={{0,1},{1,0},{2,3},{3,2},{4,5},{5,4},{6,7},{7,6},{8,9},{9,8},{10,11... | collective-permute-start | bytes 196616 | tf_op jit(solution)/shard_map/ppermute | solution.py:36
  154.5 6.2 %collective-permute-start.9 = (f32[64,256]{1,0:T(8,128)S(1)}, f32[64,256]{1,0:T(8,128)S(1)}, u32[]{:S(2)}, u32[]{:S(2)}) collective-permute-start(f32[64,256]{1,0:T(8,128)S(1)} %add.253), channel_id=1, source_target_pairs={{0,2},{1,3},{2,0},{3,1},{4,6},{5,7},{6,4},{7,5},{8,10},{9,11},{10,... | collective-permute-start | bytes 196616 | tf_op jit(solution)/shard_map/ppermute | solution.py:36
  160.7 7.8 %collective-permute-start.10 = (f32[64,256]{1,0:T(8,128)S(1)}, f32[64,256]{1,0:T(8,128)S(1)}, u32[]{:S(2)}, u32[]{:S(2)}) collective-permute-start(f32[64,256]{1,0:T(8,128)S(1)} %add.254), channel_id=1, source_target_pairs={{0,4},{1,5},{2,6},{3,7},{4,0},{5,1},{6,2},{7,3},{8,12},{9,13},{10,... | collective-permute-start | bytes 196616 | tf_op jit(solution)/shard_map/ppermute | solution.py:36
  168.5 13.6 %collective-permute-start.11 = (f32[64,256]{1,0:T(8,128)S(1)}, f32[64,256]{1,0:T(8,128)S(1)}, u32[]{:S(2)}, u32[]{:S(2)}) collective-permute-start(f32[64,256]{1,0:T(8,128)S(1)} %add.255), channel_id=1, source_target_pairs={{0,8},{1,9},{2,10},{3,11},{4,12},{5,13},{6,14},{7,15},{8,0},{9,1},... | collective-permute-start | bytes 196616 | tf_op jit(solution)/shard_map/ppermute | solution.py:36
  182.0 6.9 %collective-permute-start.12 = (f32[64,256]{1,0:T(8,128)S(1)}, f32[64,256]{1,0:T(8,128)S(1)}, u32[]{:S(2)}, u32[]{:S(2)}) collective-permute-start(f32[64,256]{1,0:T(8,128)S(1)} %add.256), channel_id=1, source_target_pairs={{0,16},{1,17},{2,18},{3,19},{4,20},{5,21},{6,22},{7,23},{8,24},{9,... | collective-permute-start | bytes 196616 | tf_op jit(solution)/shard_map/ppermute | solution.py:36
  188.9 7.1 %collective-permute-start.13 = (f32[64,256]{1,0:T(8,128)S(1)}, f32[64,256]{1,0:T(8,128)S(1)}, u32[]{:S(2)}, u32[]{:S(2)}) collective-permute-start(f32[64,256]{1,0:T(8,128)S(1)} %add.257), channel_id=1, source_target_pairs={{0,32},{1,33},{2,34},{3,35},{4,36},{5,37},{6,38},{7,39},{8,40},{9,... | collective-permute-start | bytes 196616 | tf_op jit(solution)/shard_map/ppermute | solution.py:36
  196.0 10.8 %collective-permute-start.14 = (f32[64,256]{1,0:T(8,128)S(1)}, f32[64,256]{1,0:T(8,128)S(1)}, u32[]{:S(2)}, u32[]{:S(2)}) collective-permute-start(f32[64,256]{1,0:T(8,128)S(1)} %add.258), channel_id=1, source_target_pairs={{0,64},{1,65},{2,66},{3,67},{4,68},{5,69},{6,70},{7,71},{8,72},{9,... | collective-permute-start | bytes 196616 | tf_op jit(solution)/shard_map/ppermute | solution.py:36
  209.9 7.7 %collective-permute-start.16 = (f32[64,256]{1,0:T(8,128)S(1)}, f32[64,256]{1,0:T(8,128)S(1)}, u32[]{:S(2)}, u32[]{:S(2)}) collective-permute-start(f32[64,256]{1,0:T(8,128)S(1)} %add.260), channel_id=1, source_target_pairs={{0,256},{1,257},{2,258},{3,259},{4,260},{5,261},{6,262},{7,263},{8... | collective-permute-start | bytes 196616 | tf_op jit(solution)/shard_map/ppermute | solution.py:36
  224.2 6.2 %collective-permute-start.17 = (f32[64,256]{1,0:T(8,128)S(1)}, f32[64,256]{1,0:T(8,128)S(1)}, u32[]{:S(2)}, u32[]{:S(2)}) collective-permute-start(f32[64,256]{1,0:T(8,128)S(1)} %fusion.69), channel_id=1, source_target_pairs={{0,1},{1,0},{2,3},{3,2},{4,5},{5,4},{6,7},{7,6},{8,9},{9,8},{10,11... | collective-permute-start | bytes 196616 | tf_op jit(solution)/shard_map/ppermute | solution.py:36
  230.3 6.2 %collective-permute-start.18 = (f32[64,256]{1,0:T(8,128)S(1)}, f32[64,256]{1,0:T(8,128)S(1)}, u32[]{:S(2)}, u32[]{:S(2)}) collective-permute-start(f32[64,256]{1,0:T(8,128)S(1)} %add.262), channel_id=1, source_target_pairs={{0,2},{1,3},{2,0},{3,1},{4,6},{5,7},{6,4},{7,5},{8,10},{9,11},{10,... | collective-permute-start | bytes 196616 | tf_op jit(solution)/shard_map/ppermute | solution.py:36
  236.5 7.2 %collective-permute-start.19 = (f32[64,256]{1,0:T(8,128)S(1)}, f32[64,256]{1,0:T(8,128)S(1)}, u32[]{:S(2)}, u32[]{:S(2)}) collective-permute-start(f32[64,256]{1,0:T(8,128)S(1)} %add.263), channel_id=1, source_target_pairs={{0,4},{1,5},{2,6},{3,7},{4,0},{5,1},{6,2},{7,3},{8,12},{9,13},{10,... | collective-permute-start | bytes 196616 | tf_op jit(solution)/shard_map/ppermute | solution.py:36
  243.7 10.2 %collective-permute-start.20 = (f32[64,256]{1,0:T(8,128)S(1)}, f32[64,256]{1,0:T(8,128)S(1)}, u32[]{:S(2)}, u32[]{:S(2)}) collective-permute-start(f32[64,256]{1,0:T(8,128)S(1)} %add.264), channel_id=1, source_target_pairs={{0,8},{1,9},{2,10},{3,11},{4,12},{5,13},{6,14},{7,15},{8,0},{9,1},... | collective-permute-start | bytes 196616 | tf_op jit(solution)/shard_map/ppermute | solution.py:36
  254.0 6.7 %collective-permute-start.21 = (f32[64,256]{1,0:T(8,128)S(1)}, f32[64,256]{1,0:T(8,128)S(1)}, u32[]{:S(2)}, u32[]{:S(2)}) collective-permute-start(f32[64,256]{1,0:T(8,128)S(1)} %add.265), channel_id=1, source_target_pairs={{0,16},{1,17},{2,18},{3,19},{4,20},{5,21},{6,22},{7,23},{8,24},{9,... | collective-permute-start | bytes 196616 | tf_op jit(solution)/shard_map/ppermute | solution.py:36
  260.7 7.8 %collective-permute-start.22 = (f32[64,256]{1,0:T(8,128)S(1)}, f32[64,256]{1,0:T(8,128)S(1)}, u32[]{:S(2)}, u32[]{:S(2)}) collective-permute-start(f32[64,256]{1,0:T(8,128)S(1)} %add.266), channel_id=1, source_target_pairs={{0,32},{1,33},{2,34},{3,35},{4,36},{5,37},{6,38},{7,39},{8,40},{9,... | collective-permute-start | bytes 196616 | tf_op jit(solution)/shard_map/ppermute | solution.py:36
  268.5 10.1 %collective-permute-start.23 = (f32[64,256]{1,0:T(8,128)S(1)}, f32[64,256]{1,0:T(8,128)S(1)}, u32[]{:S(2)}, u32[]{:S(2)}) collective-permute-start(f32[64,256]{1,0:T(8,128)S(1)} %add.267), channel_id=1, source_target_pairs={{0,64},{1,65},{2,66},{3,67},{4,68},{5,69},{6,70},{7,71},{8,72},{9,... | collective-permute-start | bytes 196616 | tf_op jit(solution)/shard_map/ppermute | solution.py:36
  281.7 7.7 %collective-permute-start.25 = (f32[64,256]{1,0:T(8,128)S(1)}, f32[64,256]{1,0:T(8,128)S(1)}, u32[]{:S(2)}, u32[]{:S(2)}) collective-permute-start(f32[64,256]{1,0:T(8,128)S(1)} %add.269), channel_id=1, source_target_pairs={{0,256},{1,257},{2,258},{3,259},{4,260},{5,261},{6,262},{7,263},{8... | collective-permute-start | bytes 196616 | tf_op jit(solution)/shard_map/ppermute | solution.py:36
  293.0 5.8 %collective-permute-start.26 = (f32[64,64]{0,1:T(8,128)S(1)}, f32[64,64]{0,1:T(8,128)S(1)}, u32[]{:S(2)}, u32[]{:S(2)}) collective-permute-start(f32[64,64]{0,1:T(8,128)S(1)} %fusion.70), channel_id=1, source_target_pairs={{0,1},{1,0},{2,3},{3,2},{4,5},{5,4},{6,7},{7,6},{8,9},{9,8},{10,11... | collective-permute-start | bytes 49160 | tf_op jit(solution)/shard_map/ppermute | solution.py:36
  304.7 6.9 %collective-permute-start.28 = (f32[64,64]{0,1:T(8,128)S(1)}, f32[64,64]{0,1:T(8,128)S(1)}, u32[]{:S(2)}, u32[]{:S(2)}) collective-permute-start(f32[64,64]{0,1:T(8,128)S(1)} %add.272), channel_id=1, source_target_pairs={{0,4},{1,5},{2,6},{3,7},{4,0},{5,1},{6,2},{7,3},{8,12},{9,13},{10,... | collective-permute-start | bytes 49160 | tf_op jit(solution)/shard_map/ppermute | solution.py:36
  311.6 9.7 %collective-permute-start.29 = (f32[64,64]{0,1:T(8,128)S(1)}, f32[64,64]{0,1:T(8,128)S(1)}, u32[]{:S(2)}, u32[]{:S(2)}) collective-permute-start(f32[64,64]{0,1:T(8,128)S(1)} %add.273), channel_id=1, source_target_pairs={{0,8},{1,9},{2,10},{3,11},{4,12},{5,13},{6,14},{7,15},{8,0},{9,1},... | collective-permute-start | bytes 49160 | tf_op jit(solution)/shard_map/ppermute | solution.py:36
  327.1 6.8 %collective-permute-start.31 = (f32[64,64]{0,1:T(8,128)S(1)}, f32[64,64]{0,1:T(8,128)S(1)}, u32[]{:S(2)}, u32[]{:S(2)}) collective-permute-start(f32[64,64]{0,1:T(8,128)S(1)} %add.275), channel_id=1, source_target_pairs={{0,32},{1,33},{2,34},{3,35},{4,36},{5,37},{6,38},{7,39},{8,40},{9,... | collective-permute-start | bytes 49160 | tf_op jit(solution)/shard_map/ppermute | solution.py:36
  333.9 9.7 %collective-permute-start.32 = (f32[64,64]{0,1:T(8,128)S(1)}, f32[64,64]{0,1:T(8,128)S(1)}, u32[]{:S(2)}, u32[]{:S(2)}) collective-permute-start(f32[64,64]{0,1:T(8,128)S(1)} %add.276), channel_id=1, source_target_pairs={{0,64},{1,65},{2,66},{3,67},{4,68},{5,69},{6,70},{7,71},{8,72},{9,... | collective-permute-start | bytes 49160 | tf_op jit(solution)/shard_map/ppermute | solution.py:36
  346.7 7.3 %collective-permute-start.34 = (f32[64,64]{0,1:T(8,128)S(1)}, f32[64,64]{0,1:T(8,128)S(1)}, u32[]{:S(2)}, u32[]{:S(2)}) collective-permute-start(f32[64,64]{0,1:T(8,128)S(1)} %add.278), channel_id=1, source_target_pairs={{0,256},{1,257},{2,258},{3,259},{4,260},{5,261},{6,262},{7,263},{8... | collective-permute-start | bytes 49160 | tf_op jit(solution)/shard_map/ppermute | solution.py:36
  (10 other events, 137.1 us)
where the time goes:
time: 371 us; the launch traced here: 370 us
  waiting for transfers between devices  167 us (45%)
  starting transfers between devices  145 us (39%)
  other arithmetic  23.4 us (6%)
  matrix products  18.1 us (5%)
  local copies, waits for them, and re-layouts  15.3 us (4%)
    ppermute x27, waiting for transfers between devices, allsum(): lax.ppermute(value, axes, [(i, i ^ mask) for i in range(total)])  104 us
    ppermute x27, starting transfers between devices, allsum(): lax.ppermute(value, axes, [(i, i ^ mask) for i in range(total)])  89.7 us
    ppermute x4, starting transfers between devices, padded_2(): lax.ppermute(head, axis, [((i + 1) % count, i) for i in range(ends)])  38.4 us
    ppermute x4, waiting for transfers between devices, padded_2(): lax.ppermute(tail, axis, [(i, (i + 1) % count) for i in range(ends)])  36.4 us
    ppermute x4, waiting for transfers between devices, padded_2(): lax.ppermute(head, axis, [((i + 1) % count, i) for i in range(ends)])  17.1 us
    dot_general x3, matrix products, products(): lax.dot_general(left_side, right_side, (((1,), (1,)), ((), ())), precisio...  11.2 us
    unnamed x13, local copies, waits for them, and re-layouts  9.6 us
    ppermute x4, starting transfers between devices, padded_2(): lax.ppermute(tail, axis, [(i, (i + 1) % count) for i in range(ends)])  9.09 us
  transfers between devices with their start and end apart: 37, of which 37 were waited for; matrix products, arithmetic and copies ran while one was open for 3% of the time, Pallas kernels for 0%

commit v1 on v0

--- a/solution.py
+++ b/solution.py
@@ -7,6 +7,12 @@
 SWEEPS = 4
 LOWER_BOUND = 0.1
 UPPER_BOUND = 2.0
+
+
+def stacked_exchange(x, axis, split, join):
+    cells = jnp.split(x, lax.axis_size(axis), axis=split)
+    received = lax.all_to_all(jnp.stack(cells), axis, 0, 0)
+    return jnp.concatenate(received, axis=join)
 
 
 def padded_2(cells, sides, width):
@@ -137,7 +143,7 @@
 
     fields = chebyshev(source, face_list, diagonal, padder)
     merged = fields.reshape(per_device * COLS, slab_x, full_y, depth)
-    regrouped = lax.all_to_all(merged, "shift", split_axis=2, concat_axis=0, tiled=True)
+    regrouped = stacked_exchange(merged, "shift", 2, 0)
     columns = regrouped.reshape(new_count, slab_x * quarter * depth)
     first_proj = allsum(products(columns, flat_basis)) * cell_weight
     columns = columns - matmul(first_proj, flat_basis)

time: 371 us -> 370 us (level)
  no operation moved by 1% of the time
where the time goes in v1:
time: 370 us; the launch traced here: 368 us
  waiting for transfers between devices  167 us (45%)
  starting transfers between devices  145 us (39%)
  other arithmetic  24.4 us (7%)
  matrix products  18.1 us (5%)
  local copies, waits for them, and re-layouts  12.9 us (3%)
    ppermute x27, waiting for transfers between devices, allsum(): lax.ppermute(value, axes, [(i, i ^ mask) for i in range(total)])  104 us
    ppermute x27, starting transfers between devices, allsum(): lax.ppermute(value, axes, [(i, i ^ mask) for i in range(total)])  89.8 us
    ppermute x4, starting transfers between devices, padded_2(): lax.ppermute(head, axis, [((i + 1) % count, i) for i in range(ends)])  38.4 us
    ppermute x4, waiting for transfers between devices, padded_2(): lax.ppermute(tail, axis, [(i, (i + 1) % count) for i in range(ends)])  36.4 us
    ppermute x4, waiting for transfers between devices, padded_2(): lax.ppermute(head, axis, [((i + 1) % count, i) for i in range(ends)])  17.1 us
    dot_general x3, matrix products, products(): lax.dot_general(left_side, right_side, (((1,), (1,)), ((), ())), precisio...  11.2 us
    unnamed x13, local copies, waits for them, and re-layouts  9.59 us
    ppermute x4, starting transfers between devices, padded_2(): lax.ppermute(tail, axis, [(i, (i + 1) % count) for i in range(ends)])  9.09 us
  transfers between devices with their start and end apart: 37, of which 37 were waited for; matrix products, arithmetic and copies ran while one was open for 3% of the time, Pallas kernels for 0%

profile of v1, /device:TPU:56, one launch (start us, length us, event | category | flops | bytes accessed | tf_op | source)
XLA Modules:
  0.0 368.5 jit_solution(163243185408543665)
XLA Ops:
  3.0 4.3 %all-to-all-start = ((f32[64,2,8,256]{3,2,1,0:T(8,128)}), f32[64,2,8,256]{3,2,1,0:T(8,128)S(1)}, u32[]{:S(2)}, u32[]{:S(2)}) async-start(f32[64,2,8,256]{3,2,1,0:T(8,128)} %slice.133), calls=%async_computation | async-start | bytes 2097152 | tf_op jit(solution)/shard_map/all_to_all | solution.py:136
  10.1 11.2 %collective-permute-start.1 = (f32[1,32,256]{2,1,0:T(8,128)S(1)}, f32[1,32,256]{2,1,0:T(8,128)S(1)}, u32[]{:S(2)}, u32[]{:S(2)}) collective-permute-start(f32[1,32,256]{2,1,0:T(8,128)S(1)} %get-tuple-element.44), channel_id=1, source_target_pairs={{1,0},{2,1},{3,2},{4,3},{5,4},{6,5},{7,6},{8,7},{9,8},{10,9},{11,1... | collective-permute-start | bytes 98312 | tf_op jit(solution)/shard_map/ppermute | solution.py:28
  27.3 11.2 %collective-permute-start.3 = (f32[2,8,1,32,256]{4,3,2,1,0:T(8,128)S(1)}, f32[2,8,1,32,256]{4,3,2,1,0:T(8,128)S(1)}, u32[]{:S(2)}, u32[]{:S(2)}) collective-permute-start(f32[2,8,1,32,256]{4,3,2,1,0:T(8,128)S(1)} %get-tuple-element.39), channel_id=1, source_target_pairs={{1,0},{2,1},{3,2},{4,3},{5,4},{6,5},{7,6},{8,7},{9,8},{10,9},{11,1... | collective-permute-start | bytes 1572872 | tf_op jit(solution)/shard_map/ppermute | solution.py:28
  38.5 10.3 %collective-permute-done.2 = f32[2,8,1,32,256]{4,3,2,1,0:T(8,128)S(1)} collective-permute-done((f32[2,8,1,32,256]{4,3,2,1,0:T(8,128)S(1)}, f32[2,8,1,32,256]{4,3,2,1,0:T(8,128)S(1)}, u32[]{:S(2)}, u32[]{:S(2)}) %collective-permute-start.2) | collective-permute-done | bytes 524320 | tf_op jit(solution)/shard_map/ppermute | solution.py:26
  48.7 5.9 %collective-permute-done.3 = f32[2,8,1,32,256]{4,3,2,1,0:T(8,128)S(1)} collective-permute-done((f32[2,8,1,32,256]{4,3,2,1,0:T(8,128)S(1)}, f32[2,8,1,32,256]{4,3,2,1,0:T(8,128)S(1)}, u32[]{:S(2)}, u32[]{:S(2)}) %collective-permute-start.3) | collective-permute-done | bytes 524320 | tf_op jit(solution)/shard_map/ppermute | solution.py:28
  59.7 8.1 %collective-permute-start.5 = (f32[2,8,1,32,256]{4,3,2,1,0:T(8,128)S(1)}, f32[2,8,1,32,256]{4,3,2,1,0:T(8,128)S(1)}, u32[]{:S(2)}, u32[]{:S(2)}) collective-permute-start(f32[2,8,1,32,256]{4,3,2,1,0:T(8,128)S(1)} %get-tuple-element.37), channel_id=1, source_target_pairs={{1,0},{2,1},{3,2},{4,3},{5,4},{6,5},{7,6},{8,7},{9,8},{10,9},{11,1... | collective-permute-start | bytes 1572872 | tf_op jit(solution)/shard_map/ppermute | solution.py:28
  67.9 13.1 %collective-permute-done.4 = f32[2,8,1,32,256]{4,3,2,1,0:T(8,128)S(1)} collective-permute-done((f32[2,8,1,32,256]{4,3,2,1,0:T(8,128)S(1)}, f32[2,8,1,32,256]{4,3,2,1,0:T(8,128)S(1)}, u32[]{:S(2)}, u32[]{:S(2)}) %collective-permute-start.4) | collective-permute-done | bytes 524320 | tf_op jit(solution)/shard_map/ppermute | solution.py:26
  80.9 4.7 %collective-permute-done.5 = f32[2,8,1,32,256]{4,3,2,1,0:T(8,128)S(1)} collective-permute-done((f32[2,8,1,32,256]{4,3,2,1,0:T(8,128)S(1)}, f32[2,8,1,32,256]{4,3,2,1,0:T(8,128)S(1)}, u32[]{:S(2)}, u32[]{:S(2)}) %collective-permute-start.5) | collective-permute-done | bytes 524320 | tf_op jit(solution)/shard_map/ppermute | solution.py:28
  90.7 7.9 %collective-permute-start.7 = (f32[2,8,1,32,256]{4,3,2,1,0:T(8,128)S(1)}, f32[2,8,1,32,256]{4,3,2,1,0:T(8,128)S(1)}, u32[]{:S(2)}, u32[]{:S(2)}) collective-permute-start(f32[2,8,1,32,256]{4,3,2,1,0:T(8,128)S(1)} %get-tuple-element.35), channel_id=1, source_target_pairs={{1,0},{2,1},{3,2},{4,3},{5,4},{6,5},{7,6},{8,7},{9,8},{10,9},{11,1... | collective-permute-start | bytes 1572872 | tf_op jit(solution)/shard_map/ppermute | solution.py:28
  98.6 13.0 %collective-permute-done.6 = f32[2,8,1,32,256]{4,3,2,1,0:T(8,128)S(1)} collective-permute-done((f32[2,8,1,32,256]{4,3,2,1,0:T(8,128)S(1)}, f32[2,8,1,32,256]{4,3,2,1,0:T(8,128)S(1)}, u32[]{:S(2)}, u32[]{:S(2)}) %collective-permute-start.6) | collective-permute-done | bytes 524320 | tf_op jit(solution)/shard_map/ppermute | solution.py:26
  111.6 5.0 %collective-permute-done.7 = f32[2,8,1,32,256]{4,3,2,1,0:T(8,128)S(1)} collective-permute-done((f32[2,8,1,32,256]{4,3,2,1,0:T(8,128)S(1)}, f32[2,8,1,32,256]{4,3,2,1,0:T(8,128)S(1)}, u32[]{:S(2)}, u32[]{:S(2)}) %collective-permute-start.7) | collective-permute-done | bytes 524320 | tf_op jit(solution)/shard_map/ppermute | solution.py:28
  124.7 8.0 %copy.36 = f32[32,8,16,256]{3,1,2,0:T(8,128)} copy(f32[32,8,16,256]{3,2,1,0:T(8,128)} %bitcast.56) | data formatting | bytes 8388608
  132.7 7.8 %all-to-all-done.1 = f32[4,16,2,8,256]{4,3,2,1,0:T(8,128)S(1)} async-done(((f32[4,16,2,8,256]{4,3,2,1,0:T(8,128)}), f32[4,16,2,8,256]{4,3,2,1,0:T(8,128)S(1)}, u32[]{:S(2)}, u32[]{:S(2)}) %all-to-all-start.1) | async-done | bytes 1048608 | tf_op jit(solution)/shard_map/all_to_all | solution.py:14
  140.7 6.3 %fusion.68 = f32[64,256]{1,0:T(8,128)S(1)} fusion(f32[64,4096]{1,0:T(8,128)S(1)} %reshape_reshape.3, f32[256,4096]{1,0:T(8,128)} %bitcast.48), kind=kOutput, calls=%fused_computation.125 | convolution fusion | flops 805306368 | bytes 5308416 | tf_op jit(solution)/shard_map/dot_general | solution.py:107
  148.9 4.2 %collective-permute-done.8 = f32[64,256]{1,0:T(8,128)S(1)} collective-permute-done((f32[64,256]{1,0:T(8,128)S(1)}, f32[64,256]{1,0:T(8,128)S(1)}, u32[]{:S(2)}, u32[]{:S(2)}) %collective-permute-start.8) | collective-permute-done | bytes 65568 | tf_op jit(solution)/shard_map/ppermute | solution.py:42
  155.1 4.2 %collective-permute-done.9 = f32[64,256]{1,0:T(8,128)S(1)} collective-permute-done((f32[64,256]{1,0:T(8,128)S(1)}, f32[64,256]{1,0:T(8,128)S(1)}, u32[]{:S(2)}, u32[]{:S(2)}) %collective-permute-start.9) | collective-permute-done | bytes 65568 | tf_op jit(solution)/shard_map/ppermute | solution.py:42
  162.8 4.3 %collective-permute-done.10 = f32[64,256]{1,0:T(8,128)S(1)} collective-permute-done((f32[64,256]{1,0:T(8,128)S(1)}, f32[64,256]{1,0:T(8,128)S(1)}, u32[]{:S(2)}, u32[]{:S(2)}) %collective-permute-start.10) | collective-permute-done | bytes 65568 | tf_op jit(solution)/shard_map/ppermute | solution.py:42
  167.1 11.3 %collective-permute-start.11 = (f32[64,256]{1,0:T(8,128)S(1)}, f32[64,256]{1,0:T(8,128)S(1)}, u32[]{:S(2)}, u32[]{:S(2)}) collective-permute-start(f32[64,256]{1,0:T(8,128)S(1)} %add.255), channel_id=1, source_target_pairs={{0,8},{1,9},{2,10},{3,11},{4,12},{5,13},{6,14},{7,15},{8,0},{9,1},... | collective-permute-start | bytes 196616 | tf_op jit(solution)/shard_map/ppermute | solution.py:42
  194.6 4.8 %collective-permute-start.14 = (f32[64,256]{1,0:T(8,128)S(1)}, f32[64,256]{1,0:T(8,128)S(1)}, u32[]{:S(2)}, u32[]{:S(2)}) collective-permute-start(f32[64,256]{1,0:T(8,128)S(1)} %add.258), channel_id=1, source_target_pairs={{0,64},{1,65},{2,66},{3,67},{4,68},{5,69},{6,70},{7,71},{8,72},{9,... | collective-permute-start | bytes 196616 | tf_op jit(solution)/shard_map/ppermute | solution.py:42
  199.4 5.9 %collective-permute-done.14 = f32[64,256]{1,0:T(8,128)S(1)} collective-permute-done((f32[64,256]{1,0:T(8,128)S(1)}, f32[64,256]{1,0:T(8,128)S(1)}, u32[]{:S(2)}, u32[]{:S(2)}) %collective-permute-start.14) | collective-permute-done | bytes 65568 | tf_op jit(solution)/shard_map/ppermute | solution.py:42
  211.1 5.1 %collective-permute-done.16 = f32[64,256]{1,0:T(8,128)S(1)} collective-permute-done((f32[64,256]{1,0:T(8,128)S(1)}, f32[64,256]{1,0:T(8,128)S(1)}, u32[]{:S(2)}, u32[]{:S(2)}) %collective-permute-start.16) | collective-permute-done | bytes 65568 | tf_op jit(solution)/shard_map/ppermute | solution.py:42
  230.9 4.2 %collective-permute-done.18 = f32[64,256]{1,0:T(8,128)S(1)} collective-permute-done((f32[64,256]{1,0:T(8,128)S(1)}, f32[64,256]{1,0:T(8,128)S(1)}, u32[]{:S(2)}, u32[]{:S(2)}) %collective-permute-start.18) | collective-permute-done | bytes 65568 | tf_op jit(solution)/shard_map/ppermute | solution.py:42
  237.1 5.3 %collective-permute-done.19 = f32[64,256]{1,0:T(8,128)S(1)} collective-permute-done((f32[64,256]{1,0:T(8,128)S(1)}, f32[64,256]{1,0:T(8,128)S(1)}, u32[]{:S(2)}, u32[]{:S(2)}) %collective-permute-start.19) | collective-permute-done | bytes 65568 | tf_op jit(solution)/shard_map/ppermute | solution.py:42
  242.4 8.0 %collective-permute-start.20 = (f32[64,256]{1,0:T(8,128)S(1)}, f32[64,256]{1,0:T(8,128)S(1)}, u32[]{:S(2)}, u32[]{:S(2)}) collective-permute-start(f32[64,256]{1,0:T(8,128)S(1)} %add.264), channel_id=1, source_target_pairs={{0,8},{1,9},{2,10},{3,11},{4,12},{5,13},{6,14},{7,15},{8,0},{9,1},... | collective-permute-start | bytes 196616 | tf_op jit(solution)/shard_map/ppermute | solution.py:42
  262.7 4.4 %collective-permute-done.22 = f32[64,256]{1,0:T(8,128)S(1)} collective-permute-done((f32[64,256]{1,0:T(8,128)S(1)}, f32[64,256]{1,0:T(8,128)S(1)}, u32[]{:S(2)}, u32[]{:S(2)}) %collective-permute-start.22) | collective-permute-done | bytes 65568 | tf_op jit(solution)/shard_map/ppermute | solution.py:42
  270.8 6.4 %collective-permute-done.23 = f32[64,256]{1,0:T(8,128)S(1)} collective-permute-done((f32[64,256]{1,0:T(8,128)S(1)}, f32[64,256]{1,0:T(8,128)S(1)}, u32[]{:S(2)}, u32[]{:S(2)}) %collective-permute-start.23) | collective-permute-done | bytes 65568 | tf_op jit(solution)/shard_map/ppermute | solution.py:42
  282.9 5.2 %collective-permute-done.25 = f32[64,256]{1,0:T(8,128)S(1)} collective-permute-done((f32[64,256]{1,0:T(8,128)S(1)}, f32[64,256]{1,0:T(8,128)S(1)}, u32[]{:S(2)}, u32[]{:S(2)}) %collective-permute-start.25) | collective-permute-done | bytes 65568 | tf_op jit(solution)/shard_map/ppermute | solution.py:42
  305.2 5.0 %collective-permute-done.28 = f32[64,64]{0,1:T(8,128)S(1)} collective-permute-done((f32[64,64]{0,1:T(8,128)S(1)}, f32[64,64]{0,1:T(8,128)S(1)}, u32[]{:S(2)}, u32[]{:S(2)}) %collective-permute-start.28) | collective-permute-done | bytes 16416 | tf_op jit(solution)/shard_map/ppermute | solution.py:42
  310.2 7.6 %collective-permute-start.29 = (f32[64,64]{0,1:T(8,128)S(1)}, f32[64,64]{0,1:T(8,128)S(1)}, u32[]{:S(2)}, u32[]{:S(2)}) collective-permute-start(f32[64,64]{0,1:T(8,128)S(1)} %add.273), channel_id=1, source_target_pairs={{0,8},{1,9},{2,10},{3,11},{4,12},{5,13},{6,14},{7,15},{8,0},{9,1},... | collective-permute-start | bytes 49160 | tf_op jit(solution)/shard_map/ppermute | solution.py:42
  336.2 6.0 %collective-permute-done.32 = f32[64,64]{0,1:T(8,128)S(1)} collective-permute-done((f32[64,64]{0,1:T(8,128)S(1)}, f32[64,64]{0,1:T(8,128)S(1)}, u32[]{:S(2)}, u32[]{:S(2)}) %collective-permute-start.32) | collective-permute-done | bytes 16416 | tf_op jit(solution)/shard_map/ppermute | solution.py:42
  352.8 5.8 %cholesky.16 = f32[64,64]{1,0:T(8,128)S(1)} custom-call(f32[64,64]{1,0:T(8,128)S(1)} %fusion.52), custom_call_target="Cholesky" | custom-call | tf_op jit(solution)/shard_map/jit(cholesky)/cholesky | solution.py:153
  360.6 4.9 %custom-call.6 = f32[1,64,64]{1,2,0:T(8,128)S(1)} custom-call(f32[1,64,64]{2,1,0:T(8,128)S(1)} %get-tuple-element.17), custom_call_target="InvertDiagBlocksLowerTriangular" | custom-call | tf_op jit(solution)/shard_map/triangular_solve | solution.py:154
  (116 shorter events, 147.7 us)
Async XLA Ops:
  3.0 21.3 %all-to-all-start = ((f32[64,2,8,256]{3,2,1,0:T(8,128)}), f32[64,2,8,256]{3,2,1,0:T(8,128)S(1)}, u32[]{:S(2)}, u32[]{:S(2)}) async-start(f32[64,2,8,256]{3,2,1,0:T(8,128)} %slice.133), calls=%async_computation | async-start | bytes 2097152 | tf_op jit(solution)/shard_map/all_to_all | solution.py:136
  7.5 14.0 %collective-permute-start = (f32[1,32,256]{2,1,0:T(8,128)S(1)}, f32[1,32,256]{2,1,0:T(8,128)S(1)}, u32[]{:S(2)}, u32[]{:S(2)}) collective-permute-start(f32[1,32,256]{2,1,0:T(8,128)S(1)} %get-tuple-element.43), channel_id=1, source_target_pairs={{0,1},{1,2},{2,3},{3,4},{4,5},{5,6},{6,7},{7,8},{8,9},{9,10},{10,1... | collective-permute-start | bytes 98312 | tf_op jit(solution)/shard_map/ppermute | solution.py:26
  10.1 12.8 %collective-permute-start.1 = (f32[1,32,256]{2,1,0:T(8,128)S(1)}, f32[1,32,256]{2,1,0:T(8,128)S(1)}, u32[]{:S(2)}, u32[]{:S(2)}) collective-permute-start(f32[1,32,256]{2,1,0:T(8,128)S(1)} %get-tuple-element.44), channel_id=1, source_target_pairs={{1,0},{2,1},{3,2},{4,3},{5,4},{6,5},{7,6},{8,7},{9,8},{10,9},{11,1... | collective-permute-start | bytes 98312 | tf_op jit(solution)/shard_map/ppermute | solution.py:28
  24.7 24.1 %collective-permute-start.2 = (f32[2,8,1,32,256]{4,3,2,1,0:T(8,128)S(1)}, f32[2,8,1,32,256]{4,3,2,1,0:T(8,128)S(1)}, u32[]{:S(2)}, u32[]{:S(2)}) collective-permute-start(f32[2,8,1,32,256]{4,3,2,1,0:T(8,128)S(1)} %get-tuple-element.38), channel_id=1, source_target_pairs={{0,1},{1,2},{2,3},{3,4},{4,5},{5,6},{6,7},{7,8},{8,9},{9,10},{10,1... | collective-permute-start | bytes 1572872 | tf_op jit(solution)/shard_map/ppermute | solution.py:26
  27.3 27.4 %collective-permute-start.3 = (f32[2,8,1,32,256]{4,3,2,1,0:T(8,128)S(1)}, f32[2,8,1,32,256]{4,3,2,1,0:T(8,128)S(1)}, u32[]{:S(2)}, u32[]{:S(2)}) collective-permute-start(f32[2,8,1,32,256]{4,3,2,1,0:T(8,128)S(1)} %get-tuple-element.39), channel_id=1, source_target_pairs={{1,0},{2,1},{3,2},{4,3},{5,4},{6,5},{7,6},{8,7},{9,8},{10,9},{11,1... | collective-permute-start | bytes 1572872 | tf_op jit(solution)/shard_map/ppermute | solution.py:28
  57.8 23.1 %collective-permute-start.4 = (f32[2,8,1,32,256]{4,3,2,1,0:T(8,128)S(1)}, f32[2,8,1,32,256]{4,3,2,1,0:T(8,128)S(1)}, u32[]{:S(2)}, u32[]{:S(2)}) collective-permute-start(f32[2,8,1,32,256]{4,3,2,1,0:T(8,128)S(1)} %get-tuple-element.36), channel_id=1, source_target_pairs={{0,1},{1,2},{2,3},{3,4},{4,5},{5,6},{6,7},{7,8},{8,9},{9,10},{10,1... | collective-permute-start | bytes 1572872 | tf_op jit(solution)/shard_map/ppermute | solution.py:26
  59.7 25.9 %collective-permute-start.5 = (f32[2,8,1,32,256]{4,3,2,1,0:T(8,128)S(1)}, f32[2,8,1,32,256]{4,3,2,1,0:T(8,128)S(1)}, u32[]{:S(2)}, u32[]{:S(2)}) collective-permute-start(f32[2,8,1,32,256]{4,3,2,1,0:T(8,128)S(1)} %get-tuple-element.37), channel_id=1, source_target_pairs={{1,0},{2,1},{3,2},{4,3},{5,4},{6,5},{7,6},{8,7},{9,8},{10,9},{11,1... | collective-permute-start | bytes 1572872 | tf_op jit(solution)/shard_map/ppermute | solution.py:28
  88.8 22.8 %collective-permute-start.6 = (f32[2,8,1,32,256]{4,3,2,1,0:T(8,128)S(1)}, f32[2,8,1,32,256]{4,3,2,1,0:T(8,128)S(1)}, u32[]{:S(2)}, u32[]{:S(2)}) collective-permute-start(f32[2,8,1,32,256]{4,3,2,1,0:T(8,128)S(1)} %get-tuple-element.34), channel_id=1, source_target_pairs={{0,1},{1,2},{2,3},{3,4},{4,5},{5,6},{6,7},{7,8},{8,9},{9,10},{10,1... | collective-permute-start | bytes 1572872 | tf_op jit(solution)/shard_map/ppermute | solution.py:26
  90.7 26.0 %collective-permute-start.7 = (f32[2,8,1,32,256]{4,3,2,1,0:T(8,128)S(1)}, f32[2,8,1,32,256]{4,3,2,1,0:T(8,128)S(1)}, u32[]{:S(2)}, u32[]{:S(2)}) collective-permute-start(f32[2,8,1,32,256]{4,3,2,1,0:T(8,128)S(1)} %get-tuple-element.35), channel_id=1, source_target_pairs={{1,0},{2,1},{3,2},{4,3},{5,4},{6,5},{7,6},{8,7},{9,8},{10,9},{11,1... | collective-permute-start | bytes 1572872 | tf_op jit(solution)/shard_map/ppermute | solution.py:28
  121.0 19.5 %all-to-all-start.1 = ((f32[4,16,2,8,256]{4,3,2,1,0:T(8,128)}), f32[4,16,2,8,256]{4,3,2,1,0:T(8,128)S(1)}, u32[]{:S(2)}, u32[]{:S(2)}) async-start(f32[4,16,2,8,256]{4,3,2,1,0:T(8,128)} %pad_maximum_fusion.6), calls=%async_computation.1 | async-start | bytes 2097152 | tf_op jit(solution)/shard_map/all_to_all | solution.py:14
  147.0 6.2 %collective-permute-start.8 = (f32[64,256]{1,0:T(8,128)S(1)}, f32[64,256]{1,0:T(8,128)S(1)}, u32[]{:S(2)}, u32[]{:S(2)}) collective-permute-start(f32[64,256]{1,0:T(8,128)S(1)} %fusion.68), channel_id=1, source_target_pairs={{0,1},{1,0},{2,3},{3,2},{4,5},{5,4},{6,7},{7,6},{8,9},{9,8},{10,11... | collective-permute-start | bytes 196616 | tf_op jit(solution)/shard_map/ppermute | solution.py:42
  153.2 6.2 %collective-permute-start.9 = (f32[64,256]{1,0:T(8,128)S(1)}, f32[64,256]{1,0:T(8,128)S(1)}, u32[]{:S(2)}, u32[]{:S(2)}) collective-permute-start(f32[64,256]{1,0:T(8,128)S(1)} %add.253), channel_id=1, source_target_pairs={{0,2},{1,3},{2,0},{3,1},{4,6},{5,7},{6,4},{7,5},{8,10},{9,11},{10,... | collective-permute-start | bytes 196616 | tf_op jit(solution)/shard_map/ppermute | solution.py:42
  159.3 7.8 %collective-permute-start.10 = (f32[64,256]{1,0:T(8,128)S(1)}, f32[64,256]{1,0:T(8,128)S(1)}, u32[]{:S(2)}, u32[]{:S(2)}) collective-permute-start(f32[64,256]{1,0:T(8,128)S(1)} %add.254), channel_id=1, source_target_pairs={{0,4},{1,5},{2,6},{3,7},{4,0},{5,1},{6,2},{7,3},{8,12},{9,13},{10,... | collective-permute-start | bytes 196616 | tf_op jit(solution)/shard_map/ppermute | solution.py:42
  167.1 13.5 %collective-permute-start.11 = (f32[64,256]{1,0:T(8,128)S(1)}, f32[64,256]{1,0:T(8,128)S(1)}, u32[]{:S(2)}, u32[]{:S(2)}) collective-permute-start(f32[64,256]{1,0:T(8,128)S(1)} %add.255), channel_id=1, source_target_pairs={{0,8},{1,9},{2,10},{3,11},{4,12},{5,13},{6,14},{7,15},{8,0},{9,1},... | collective-permute-start | bytes 196616 | tf_op jit(solution)/shard_map/ppermute | solution.py:42
  180.7 6.9 %collective-permute-start.12 = (f32[64,256]{1,0:T(8,128)S(1)}, f32[64,256]{1,0:T(8,128)S(1)}, u32[]{:S(2)}, u32[]{:S(2)}) collective-permute-start(f32[64,256]{1,0:T(8,128)S(1)} %add.256), channel_id=1, source_target_pairs={{0,16},{1,17},{2,18},{3,19},{4,20},{5,21},{6,22},{7,23},{8,24},{9,... | collective-permute-start | bytes 196616 | tf_op jit(solution)/shard_map/ppermute | solution.py:42
  187.5 7.1 %collective-permute-start.13 = (f32[64,256]{1,0:T(8,128)S(1)}, f32[64,256]{1,0:T(8,128)S(1)}, u32[]{:S(2)}, u32[]{:S(2)}) collective-permute-start(f32[64,256]{1,0:T(8,128)S(1)} %add.257), channel_id=1, source_target_pairs={{0,32},{1,33},{2,34},{3,35},{4,36},{5,37},{6,38},{7,39},{8,40},{9,... | collective-permute-start | bytes 196616 | tf_op jit(solution)/shard_map/ppermute | solution.py:42
  194.6 10.8 %collective-permute-start.14 = (f32[64,256]{1,0:T(8,128)S(1)}, f32[64,256]{1,0:T(8,128)S(1)}, u32[]{:S(2)}, u32[]{:S(2)}) collective-permute-start(f32[64,256]{1,0:T(8,128)S(1)} %add.258), channel_id=1, source_target_pairs={{0,64},{1,65},{2,66},{3,67},{4,68},{5,69},{6,70},{7,71},{8,72},{9,... | collective-permute-start | bytes 196616 | tf_op jit(solution)/shard_map/ppermute | solution.py:42
  208.6 7.7 %collective-permute-start.16 = (f32[64,256]{1,0:T(8,128)S(1)}, f32[64,256]{1,0:T(8,128)S(1)}, u32[]{:S(2)}, u32[]{:S(2)}) collective-permute-start(f32[64,256]{1,0:T(8,128)S(1)} %add.260), channel_id=1, source_target_pairs={{0,256},{1,257},{2,258},{3,259},{4,260},{5,261},{6,262},{7,263},{8... | collective-permute-start | bytes 196616 | tf_op jit(solution)/shard_map/ppermute | solution.py:42
  222.8 6.2 %collective-permute-start.17 = (f32[64,256]{1,0:T(8,128)S(1)}, f32[64,256]{1,0:T(8,128)S(1)}, u32[]{:S(2)}, u32[]{:S(2)}) collective-permute-start(f32[64,256]{1,0:T(8,128)S(1)} %fusion.69), channel_id=1, source_target_pairs={{0,1},{1,0},{2,3},{3,2},{4,5},{5,4},{6,7},{7,6},{8,9},{9,8},{10,11... | collective-permute-start | bytes 196616 | tf_op jit(solution)/shard_map/ppermute | solution.py:42
  229.0 6.2 %collective-permute-start.18 = (f32[64,256]{1,0:T(8,128)S(1)}, f32[64,256]{1,0:T(8,128)S(1)}, u32[]{:S(2)}, u32[]{:S(2)}) collective-permute-start(f32[64,256]{1,0:T(8,128)S(1)} %add.262), channel_id=1, source_target_pairs={{0,2},{1,3},{2,0},{3,1},{4,6},{5,7},{6,4},{7,5},{8,10},{9,11},{10,... | collective-permute-start | bytes 196616 | tf_op jit(solution)/shard_map/ppermute | solution.py:42
  235.2 7.2 %collective-permute-start.19 = (f32[64,256]{1,0:T(8,128)S(1)}, f32[64,256]{1,0:T(8,128)S(1)}, u32[]{:S(2)}, u32[]{:S(2)}) collective-permute-start(f32[64,256]{1,0:T(8,128)S(1)} %add.263), channel_id=1, source_target_pairs={{0,4},{1,5},{2,6},{3,7},{4,0},{5,1},{6,2},{7,3},{8,12},{9,13},{10,... | collective-permute-start | bytes 196616 | tf_op jit(solution)/shard_map/ppermute | solution.py:42
  242.4 10.2 %collective-permute-start.20 = (f32[64,256]{1,0:T(8,128)S(1)}, f32[64,256]{1,0:T(8,128)S(1)}, u32[]{:S(2)}, u32[]{:S(2)}) collective-permute-start(f32[64,256]{1,0:T(8,128)S(1)} %add.264), channel_id=1, source_target_pairs={{0,8},{1,9},{2,10},{3,11},{4,12},{5,13},{6,14},{7,15},{8,0},{9,1},... | collective-permute-start | bytes 196616 | tf_op jit(solution)/shard_map/ppermute | solution.py:42
  252.6 6.7 %collective-permute-start.21 = (f32[64,256]{1,0:T(8,128)S(1)}, f32[64,256]{1,0:T(8,128)S(1)}, u32[]{:S(2)}, u32[]{:S(2)}) collective-permute-start(f32[64,256]{1,0:T(8,128)S(1)} %add.265), channel_id=1, source_target_pairs={{0,16},{1,17},{2,18},{3,19},{4,20},{5,21},{6,22},{7,23},{8,24},{9,... | collective-permute-start | bytes 196616 | tf_op jit(solution)/shard_map/ppermute | solution.py:42
  259.4 7.8 %collective-permute-start.22 = (f32[64,256]{1,0:T(8,128)S(1)}, f32[64,256]{1,0:T(8,128)S(1)}, u32[]{:S(2)}, u32[]{:S(2)}) collective-permute-start(f32[64,256]{1,0:T(8,128)S(1)} %add.266), channel_id=1, source_target_pairs={{0,32},{1,33},{2,34},{3,35},{4,36},{5,37},{6,38},{7,39},{8,40},{9,... | collective-permute-start | bytes 196616 | tf_op jit(solution)/shard_map/ppermute | solution.py:42
  267.1 10.1 %collective-permute-start.23 = (f32[64,256]{1,0:T(8,128)S(1)}, f32[64,256]{1,0:T(8,128)S(1)}, u32[]{:S(2)}, u32[]{:S(2)}) collective-permute-start(f32[64,256]{1,0:T(8,128)S(1)} %add.267), channel_id=1, source_target_pairs={{0,64},{1,65},{2,66},{3,67},{4,68},{5,69},{6,70},{7,71},{8,72},{9,... | collective-permute-start | bytes 196616 | tf_op jit(solution)/shard_map/ppermute | solution.py:42
  280.4 7.7 %collective-permute-start.25 = (f32[64,256]{1,0:T(8,128)S(1)}, f32[64,256]{1,0:T(8,128)S(1)}, u32[]{:S(2)}, u32[]{:S(2)}) collective-permute-start(f32[64,256]{1,0:T(8,128)S(1)} %add.269), channel_id=1, source_target_pairs={{0,256},{1,257},{2,258},{3,259},{4,260},{5,261},{6,262},{7,263},{8... | collective-permute-start | bytes 196616 | tf_op jit(solution)/shard_map/ppermute | solution.py:42
  303.3 6.9 %collective-permute-start.28 = (f32[64,64]{0,1:T(8,128)S(1)}, f32[64,64]{0,1:T(8,128)S(1)}, u32[]{:S(2)}, u32[]{:S(2)}) collective-permute-start(f32[64,64]{0,1:T(8,128)S(1)} %add.272), channel_id=1, source_target_pairs={{0,4},{1,5},{2,6},{3,7},{4,0},{5,1},{6,2},{7,3},{8,12},{9,13},{10,... | collective-permute-start | bytes 49160 | tf_op jit(solution)/shard_map/ppermute | solution.py:42
  310.2 9.7 %collective-permute-start.29 = (f32[64,64]{0,1:T(8,128)S(1)}, f32[64,64]{0,1:T(8,128)S(1)}, u32[]{:S(2)}, u32[]{:S(2)}) collective-permute-start(f32[64,64]{0,1:T(8,128)S(1)} %add.273), channel_id=1, source_target_pairs={{0,8},{1,9},{2,10},{3,11},{4,12},{5,13},{6,14},{7,15},{8,0},{9,1},... | collective-permute-start | bytes 49160 | tf_op jit(solution)/shard_map/ppermute | solution.py:42
  319.9 5.8 %collective-permute-start.30 = (f32[64,64]{0,1:T(8,128)S(1)}, f32[64,64]{0,1:T(8,128)S(1)}, u32[]{:S(2)}, u32[]{:S(2)}) collective-permute-start(f32[64,64]{0,1:T(8,128)S(1)} %add.274), channel_id=1, source_target_pairs={{0,16},{1,17},{2,18},{3,19},{4,20},{5,21},{6,22},{7,23},{8,24},{9,... | collective-permute-start | bytes 49160 | tf_op jit(solution)/shard_map/ppermute | solution.py:42
  325.7 6.8 %collective-permute-start.31 = (f32[64,64]{0,1:T(8,128)S(1)}, f32[64,64]{0,1:T(8,128)S(1)}, u32[]{:S(2)}, u32[]{:S(2)}) collective-permute-start(f32[64,64]{0,1:T(8,128)S(1)} %add.275), channel_id=1, source_target_pairs={{0,32},{1,33},{2,34},{3,35},{4,36},{5,37},{6,38},{7,39},{8,40},{9,... | collective-permute-start | bytes 49160 | tf_op jit(solution)/shard_map/ppermute | solution.py:42
  332.6 9.7 %collective-permute-start.32 = (f32[64,64]{0,1:T(8,128)S(1)}, f32[64,64]{0,1:T(8,128)S(1)}, u32[]{:S(2)}, u32[]{:S(2)}) collective-permute-start(f32[64,64]{0,1:T(8,128)S(1)} %add.276), channel_id=1, source_target_pairs={{0,64},{1,65},{2,66},{3,67},{4,68},{5,69},{6,70},{7,71},{8,72},{9,... | collective-permute-start | bytes 49160 | tf_op jit(solution)/shard_map/ppermute | solution.py:42
  345.4 7.3 %collective-permute-start.34 = (f32[64,64]{0,1:T(8,128)S(1)}, f32[64,64]{0,1:T(8,128)S(1)}, u32[]{:S(2)}, u32[]{:S(2)}) collective-permute-start(f32[64,64]{0,1:T(8,128)S(1)} %add.278), channel_id=1, source_target_pairs={{0,256},{1,257},{2,258},{3,259},{4,260},{5,261},{6,262},{7,263},{8... | collective-permute-start | bytes 49160 | tf_op jit(solution)/shard_map/ppermute | solution.py:42
  (10 other events, 137.1 us)
